TPU v7x, 32 devices: a whole 2x2x4 slice. The times are simulated.
32 devices in a mesh: stream: 4 (over y, core), cross: 2 (over x), gore: 4 (over z).
Axes of the slice: x: 2, y: 2, z: 4, core: 2. Of those that a mesh axis runs over, the one named last changes fastest.
Arguments:
- density: float32 [16, 8, 512], P('stream', 'cross', 'gore'), may hold values from 1 to 2
- momentum_energy: float32 [4, 16, 8, 512], P(None, 'stream', 'cross', 'gore'), may hold values from -6 to 6
- viscosity: float32 [16, 8, 512], P('stream', 'cross', 'gore'), may hold values from 0.02 to 0.15
- records: float32 [8, 2048, 128], P(None, ('stream', 'cross', 'gore')), may hold values from -6 to 6
- cell_ids: int32 [2048, 128], P(('stream', 'cross', 'gore')), may hold values from 0 to 2047
- routes: int32 [2048, 1], P(('stream', 'cross', 'gore')), may hold values from 0 to 7; in each aligned block of 64 rows (0 to 63, 64 to 127, ...) at most 16 rows name the same one
- lengths: int32 [2048], P(('stream', 'cross', 'gore')), may hold values from 1 to 128, 163840 in all
Outputs:
- new_state: float32 [5, 16, 8, 512], P(None, 'stream', 'cross', 'gore')
- face_loads: float32 [3, 2048, 128], P(None, ('stream', 'cross', 'gore'))
Inputs may be any that keep to these rules, and one draw needn't show every extreme that they name: `routes`: among the 64 tiles of one device no fluid block is named more than 16 times, and some block exactly 16 times. `lengths`: some tile is full.
All inputs are finite; a program needn't handle non-finite values. No bound on the sum of `lengths` on one device may be relied on, other than what follows from the above.
Results may differ from a plain program's by a relative error of at most 0.0003.
Values sent between devices are 32-bit elements; how exact they have to be, the bound alone decides.
No kernel may reach another device: no remote copies, remote signals or barrier semaphores. Data moves between devices by JAX's collectives and lax.ppermute only.
A program may use at most 64 MiB of HBM per device.

v0:
```python
import jax
import jax.numpy as jnp
from jax import lax
from jax.sharding import PartitionSpec as P

SIDES = (("stream", 1), ("cross", 2), ("gore", 3))


def face_halo(block):
    wide = block
    for axis, dim in SIDES:
        count = lax.axis_size(axis)
        index = lax.axis_index(axis)
        odd = index % 2 == 1
        extent = block.shape[dim]
        last = lax.slice_in_dim(block, extent - 1, None, axis=dim)
        first = lax.slice_in_dim(block, 0, 1, axis=dim)
        pairs_a = [(i, i ^ 1) for i in range(count) if i ^ 1 < count]
        pairs_b = [
            (i, j)
            for i in range(1, count)
            for j in (i - 1, i + 1)
            if j >= 1 and j < count and (min(i, j) % 2 == 1)
        ]
        from_a = lax.ppermute(jnp.where(odd, first, last), axis, pairs_a)
        if pairs_b:
            from_b = lax.ppermute(jnp.where(odd, last, first), axis, pairs_b)
        else:
            from_b = jnp.zeros_like(from_a)
        low = jnp.where(odd, from_a, from_b)
        high = jnp.where(odd, from_b, from_a)
        widths = [(0, 0)] + [(1, 1) if d < dim else (0, 0) for d in range(1, 4)]
        wide = jnp.concatenate([jnp.pad(low, widths), wide, jnp.pad(high, widths)], axis=dim)
    return wide


def harmonic(first_visc, second_visc):
    summed = first_visc + second_visc
    denominator = jnp.where(summed > 0, summed, 1.0)
    return 2.0 * first_visc * second_visc / denominator


def shifted(values, leading, spatial, offset):
    value_portions = [slice(None)] * leading
    for position in range(3):
        extent = values.shape[leading + position]
        if position == spatial:
            value_portions.append(slice(1 + offset, extent - 1 + offset))
        else:
            value_portions.append(slice(1, extent - 1))
    return values[tuple(value_portions)]


def viscous(field, visc):
    centre = shifted(field, 1, 0, 0)
    centre_visc = shifted(visc, 0, 0, 0)
    change = jnp.zeros_like(centre)
    for spatial in range(3):
        for offset in (1, -1):
            face_visc = harmonic(centre_visc, shifted(visc, 0, spatial, offset))
            change = change + face_visc[None] * (shifted(field, 1, spatial, offset) - centre)
    return change


def split_high(values):
    scaled = values * jnp.float32(65537.0)
    high = scaled - (scaled - values)
    return (high, values - high)


def three_bf16(values):
    first, rest = split_high(values)
    second, third = split_high(rest)
    return tuple((part.astype(jnp.bfloat16) for part in (first, second, third)))


def exact_dot(spec, values, onehot, values_first):
    stacked = jnp.stack(three_bf16(values), 0)
    left, right = spec.split("->")[0].split(",")
    output = spec.split("->")[1]
    if values_first:
        terms = jnp.einsum(
            "k" + left + "," + right + "->k" + output,
            stacked,
            onehot,
            preferred_element_type=jnp.float32,
        )
    else:
        terms = jnp.einsum(
            left + ",k" + right + "->k" + output,
            onehot,
            stacked,
            preferred_element_type=jnp.float32,
        )
    return terms[0] + terms[1] + terms[2]


def shards(density, momentum_energy, viscosity, records, cell_ids, routes, lengths):
    fluid_state = jnp.concatenate([density[None], momentum_energy], 0)
    cells_x, cells_y, vertical_cells = density.shape
    plane_count = cells_x * cells_y
    tile_count = records.shape[1]
    row_count = records.shape[2]
    blocks = lax.axis_size("stream") * lax.axis_size("cross")
    capacity = max(2, 2 * tile_count // blocks)
    slot_total = blocks * capacity
    faces = slot_total * row_count
    live_rows = lax.broadcasted_iota(jnp.int32, (tile_count, row_count), 1) < lengths[:, None]
    masked_values = jnp.where(live_rows[None], records, 0.0)
    target = routes[:, 0]
    onehot = (target[:, None] == lax.broadcasted_iota(jnp.int32, (tile_count, blocks), 1)).astype(
        jnp.float32
    )
    lower = (
        lax.broadcasted_iota(jnp.int32, (tile_count, tile_count), 1)
        < lax.broadcasted_iota(jnp.int32, (tile_count, tile_count), 0)
    ).astype(jnp.float32)
    before = jnp.dot(
        lower, onehot, precision=lax.Precision.HIGHEST, preferred_element_type=jnp.float32
    )
    slot_rank = jnp.sum(before * onehot, axis=1).astype(jnp.int32)
    slot_index = target * capacity + slot_rank
    placement_plan = (
        slot_index[:, None] == lax.broadcasted_iota(jnp.int32, (tile_count, slot_total), 1)
    ).astype(jnp.float32)
    payload = jnp.concatenate(
        [jnp.abs(masked_values[0:1]), masked_values[1:5], cell_ids.astype(jnp.float32)[None]], 0
    )
    outbound = jnp.einsum("ts,ctr->csr", placement_plan, payload, precision=lax.Precision.HIGHEST)
    arrived = lax.all_to_all(outbound, ("stream", "cross"), split_axis=1, concat_axis=1, tiled=True)
    outbound, state_and_visc = lax.optimization_barrier(
        (outbound, jnp.concatenate([fluid_state, viscosity[None]], 0))
    )
    state_visc = face_halo(state_and_visc)
    state_pad = state_visc[0:5]
    visc_pad = state_visc[5]
    cells = jnp.round(arrived[5]).astype(jnp.int32).reshape(faces)
    plane = cells // vertical_cells
    depth = cells % vertical_cells
    depth_hot = depth[:, None] == lax.broadcasted_iota(jnp.int32, (faces, vertical_cells), 1)
    plane_rows = plane[None, :] == lax.broadcasted_iota(jnp.int32, (plane_count, faces), 0)
    spread = jnp.where(plane_rows[None], arrived[0:5].reshape(5, 1, faces), 0.0)
    source = jnp.einsum(
        "cpf,fd->cpd", spread, depth_hot.astype(jnp.float32), precision=lax.Precision.HIGHEST
    )
    source = source.reshape(5, cells_x, cells_y, vertical_cells)
    middle = shifted(state_pad, 1, 0, 0) + viscous(state_pad, visc_pad) + source
    middle_pad = face_halo(middle)
    new_state = middle + viscous(middle_pad, visc_pad)
    flat_state = new_state.reshape(5, plane_count, vertical_cells)
    kinetic = (
        flat_state[1] * flat_state[1]
        + flat_state[2] * flat_state[2]
        + flat_state[3] * flat_state[3]
    )
    pressure = 0.4 * (flat_state[4] - 0.5 * kinetic / flat_state[0])
    picked = exact_dot("fd,dp->fp", pressure.T, depth_hot.astype(jnp.bfloat16), False)
    plane_cols = plane[:, None] == lax.broadcasted_iota(jnp.int32, (faces, plane_count), 1)
    face_pressure = jnp.sum(jnp.where(plane_cols, picked, 0.0), axis=1)
    returned = lax.all_to_all(
        face_pressure.reshape(1, slot_total, row_count),
        ("stream", "cross"),
        split_axis=1,
        concat_axis=1,
        tiled=True,
    )
    home_pressure = jnp.einsum(
        "ts,sr->tr", placement_plan, returned[0], precision=lax.Precision.HIGHEST
    )
    face_loads = masked_values[5:8] * home_pressure[None]
    return (new_state, face_loads)


def solution(mesh):
    placed = (
        P("stream", "cross", "gore"),
        P(None, "stream", "cross", "gore"),
        P("stream", "cross", "gore"),
        P(None, ("stream", "cross", "gore"), None),
        P(("stream", "cross", "gore"), None),
        P(("stream", "cross", "gore"), None),
        P(("stream", "cross", "gore")),
    )
    return jax.shard_map(
        shards,
        mesh=mesh,
        in_specs=placed,
        out_specs=(P(None, "stream", "cross", "gore"), P(None, ("stream", "cross", "gore"), None)),
        check_vma=False,
    )
```

profile of v0, /device:TPU:0, one launch (start us, length us, event | category | flops | bytes accessed | tf_op | source)
XLA Modules:
  0.0 50.3 jit_solution(16968767982298639690)
XLA Ops:
  0.6 0.7 %iota_compare_fusion.6 = pred[64,128]{1,0:T(8,128)(4,1)S(1)} fusion(s32[64]{0:T(128)} %param.13), kind=kLoop, calls=%fused_computation.133 | loop fusion | flops 8192 | bytes 8448 | tf_op jit(solution)/shard_map/lt | solution.py:108
  1.4 1.0 %broadcast_select_fusion = f32[8,64,128]{2,1,0:T(8,128)S(1)} fusion(f32[8,64,128]{2,1,0:T(8,128)} %param.10, pred[64,128]{1,0:T(8,128)(4,1)S(1)} %iota_compare_fusion.6), kind=kLoop, calls=%fused_computation.26 | loop fusion | flops 65536 | bytes 532480 | tf_op jit(solution)/shard_map/jit(_where)/select_n | solution.py:109
  2.4 0.8 %convert_bitcast_fusion = f32[1,64,128]{2,1,0:T(8,128)S(1)} fusion(s32[64,128]{1,0:T(8,128)} %param.11), kind=kLoop, calls=%fused_computation.132 | loop fusion | flops 8192 | bytes 65536 | tf_op jit(solution)/shard_map/broadcast_in_dim | solution.py:127
  3.1 0.9 %fusion.10 = f32[64]{0:T(128)S(1)} fusion(s32[64]{0:T(128)} %bitcast.99), kind=kOutput, calls=%fused_computation.12 | convolution fusion | flops 71616 | bytes 512 | tf_op jit(solution)/shard_map/dot_general | solution.py:118
  4.0 0.7 %fusion.92 = s32[64]{0:T(128)S(1)} fusion(f32[64]{0:T(128)S(1)} %fusion.10, s32[64,1]{0,1:T(1,128)} %param.12), kind=kLoop, calls=%fused_computation.194 | loop fusion | flops 192 | bytes 768 | tf_op jit(solution)/shard_map/eq | solution.py:124
  4.7 0.5 %convolution_bitcast_fusion.1 = f32[6,128,128]{1,2,0:T(8,128)S(1)} fusion(f32[1,64,128]{2,1,0:T(8,128)S(1)} %convert_bitcast_fusion, f32[4,64,128]{2,1,0:T(8,128)S(1)} %slice.230, f32[1,64,128]{2,1,0:T(8,128)S(1)} %slice_abs_fusion, s32[64]{0:T(128)S(1)} %fusion.92), kind=kOutput, calls=%fused_computation.10 | convolution fusion | flops 75603968 | bytes 590080 | tf_op jit(solution)/shard_map/ts,ctr->csr/dot_general | solution.py:129
  5.2 1.0 %copy.11 = f32[6,128,128]{2,0,1:T(8,128)} copy(f32[6,128,128]{1,2,0:T(8,128)S(1)} %convolution_bitcast_fusion.1) | data formatting | bytes 786432 | tf_op jit(solution)/shard_map/ts,ctr->csr/transpose | solution.py:129
  6.2 5.2 %all-to-all-start = ((f32[6,128,128]{2,0,1:T(8,128)}), f32[6,128,128]{2,0,1:T(8,128)S(1)}, u32[]{:S(2)}, u32[]{:S(2)}) async-start(f32[6,128,128]{2,0,1:T(8,128)} %copy.11), calls=%async_computation | async-start | bytes 1048576 | tf_op jit(solution)/shard_map/all_to_all | solution.py:130
  11.4 0.8 %pad_maximum_fusion.6 = f32[6,4,4,128]{3,2,1,0:T(4,128)S(1)} fusion(f32[1,4,4,128]{3,2,1,0:T(4,128)} %bitcast.97, f32[4,4,4,128]{3,2,1,0:T(4,128)} %param.8, f32[1,4,4,128]{3,2,1,0:T(4,128)} %bitcast.98), kind=kLoop, calls=%fused_computation.44 | loop fusion | flops 24576 | bytes 98304 | tf_op jit(solution)/shard_map/concatenate | solution.py:132
  12.2 0.1 slice_select_fusion
  12.3 0.7 %collective-permute-start.1 = (f32[6,4,4,1]{3,2,1,0:T(4,128)S(1)}, f32[6,4,4,1]{3,2,1,0:T(4,128)S(1)}, u32[]{:S(2)}, u32[]{:S(2)}) collective-permute-start(f32[6,4,4,1]{3,2,1,0:T(4,128)S(1)} %get-tuple-element.18), channel_id=1, source_target_pairs={{1,2},{2,1},{5,6},{6,5},{9,10},{10,9},{13,14},{14,13},{17,18},{18,... | collective-permute-start | bytes 1160 | tf_op jit(solution)/shard_map/ppermute | solution.py:27
  12.9 4.5 %collective-permute-start = (f32[6,4,4,1]{3,2,1,0:T(4,128)S(1)}, f32[6,4,4,1]{3,2,1,0:T(4,128)S(1)}, u32[]{:S(2)}, u32[]{:S(2)}) collective-permute-start(f32[6,4,4,1]{3,2,1,0:T(4,128)S(1)} %get-tuple-element.19), channel_id=1, source_target_pairs={{0,1},{1,0},{2,3},{3,2},{4,5},{5,4},{6,7},{7,6},{8,9},{9,8},{10,11... | collective-permute-start | bytes 1160 | tf_op jit(solution)/shard_map/ppermute | solution.py:25
  17.4 2.1 %collective-permute-start.2 = (f32[6,4,1,128]{3,2,1,0:T(1,128)S(1)}, f32[6,4,1,128]{3,2,1,0:T(1,128)S(1)}, u32[]{:S(2)}, u32[]{:S(2)}) collective-permute-start(f32[6,4,1,128]{3,2,1,0:T(1,128)S(1)} %broadcast_select_fusion.3), channel_id=1, source_target_pairs={{0,4},{4,0},{1,5},{5,1},{2,6},{6,2},{3,7},{7,3},{8,12},{12,8},{9,1... | collective-permute-start | bytes 36872 | tf_op jit(solution)/shard_map/ppermute | solution.py:25
  19.5 0.0 collective-permute-start.3
  19.5 0.7 %collective-permute-start.4 = (f32[6,1,4,128]{3,2,1,0:T(4,128)S(1)}, f32[6,1,4,128]{3,2,1,0:T(4,128)S(1)}, u32[]{:S(2)}, u32[]{:S(2)}) collective-permute-start(f32[6,1,4,128]{3,2,1,0:T(4,128)S(1)} %get-tuple-element.17), channel_id=1, source_target_pairs={{8,16},{16,8},{9,17},{17,9},{10,18},{18,10},{11,19},{19,11},{12,20... | collective-permute-start | bytes 36872 | tf_op jit(solution)/shard_map/ppermute | solution.py:27
  20.2 0.0 collective-permute-done.1
  20.2 0.0 collective-permute-done
  20.3 0.4 collective-permute-done.3
  20.7 0.0 collective-permute-done.4
  20.7 0.5 collective-permute-done.2
  21.3 0.1 fusion.21
  21.4 0.1 fusion.77
  21.5 0.0 all-to-all-done
  21.5 0.1 slice.238
  21.6 0.1 add_select_fusion.1
  21.6 0.1 iota_compare_fusion.2
  21.8 0.5 fusion.103
  22.3 4.0 %fusion.2 = f32[5,16,128]{2,1,0:T(8,128)S(1)} fusion(s32[16384]{0:T(1024)S(1)} %get-tuple-element.9, f32[5,16,16384]{2,1,0:T(8,128)S(1)} %fusion.103), kind=kOutput, calls=%fused_computation.3 | convolution fusion | flops 2015363072 | bytes 5349376 | tf_op jit(solution)/shard_map/cpf,fd->cpd/dot_general | solution.py:143
  26.3 0.2 fusion.46
  26.5 0.1 slice_select_fusion.3
  26.6 0.7 %collective-permute-start.8 = (f32[5,4,4,1]{3,2,1,0:T(4,128)S(1)}, f32[5,4,4,1]{3,2,1,0:T(4,128)S(1)}, u32[]{:S(2)}, u32[]{:S(2)}) collective-permute-start(f32[5,4,4,1]{3,2,1,0:T(4,128)S(1)} %get-tuple-element.22), channel_id=1, source_target_pairs={{1,2},{2,1},{5,6},{6,5},{9,10},{10,9},{13,14},{14,13},{17,18},{18,... | collective-permute-start | bytes 968 | tf_op jit(solution)/shard_map/ppermute | solution.py:27
  27.3 3.7 %collective-permute-start.9 = (f32[5,4,4,1]{3,2,1,0:T(4,128)S(1)}, f32[5,4,4,1]{3,2,1,0:T(4,128)S(1)}, u32[]{:S(2)}, u32[]{:S(2)}) collective-permute-start(f32[5,4,4,1]{3,2,1,0:T(4,128)S(1)} %get-tuple-element.23), channel_id=1, source_target_pairs={{0,1},{1,0},{2,3},{3,2},{4,5},{5,4},{6,7},{7,6},{8,9},{9,8},{10,11... | collective-permute-start | bytes 968 | tf_op jit(solution)/shard_map/ppermute | solution.py:25
  31.1 0.9 %collective-permute-start.7 = (f32[5,4,1,128]{3,2,1,0:T(1,128)S(1)}, f32[5,4,1,128]{3,2,1,0:T(1,128)S(1)}, u32[]{:S(2)}, u32[]{:S(2)}) collective-permute-start(f32[5,4,1,128]{3,2,1,0:T(1,128)S(1)} %broadcast_select_fusion.10), channel_id=1, source_target_pairs={{0,4},{4,0},{1,5},{5,1},{2,6},{6,2},{3,7},{7,3},{8,12},{12,8},{9,1... | collective-permute-start | bytes 30728 | tf_op jit(solution)/shard_map/ppermute | solution.py:25
  32.0 0.5 collective-permute-start.6
  32.4 0.7 %collective-permute-start.5 = (f32[5,1,4,128]{3,2,1,0:T(4,128)S(1)}, f32[5,1,4,128]{3,2,1,0:T(4,128)S(1)}, u32[]{:S(2)}, u32[]{:S(2)}) collective-permute-start(f32[5,1,4,128]{3,2,1,0:T(4,128)S(1)} %get-tuple-element.21), channel_id=1, source_target_pairs={{8,16},{16,8},{9,17},{17,9},{10,18},{18,10},{11,19},{19,11},{12,20... | collective-permute-start | bytes 30728 | tf_op jit(solution)/shard_map/ppermute | solution.py:27
  33.1 0.0 collective-permute-done.8
  33.1 0.0 collective-permute-done.9
  33.1 1.6 %collective-permute-done.7 = f32[5,4,1,128]{3,2,1,0:T(1,128)S(1)} collective-permute-done((f32[5,4,1,128]{3,2,1,0:T(1,128)S(1)}, f32[5,4,1,128]{3,2,1,0:T(1,128)S(1)}, u32[]{:S(2)}, u32[]{:S(2)}) %collective-permute-start.7) | collective-permute-done | bytes 10272 | tf_op jit(solution)/shard_map/ppermute | solution.py:25
  34.8 0.0 collective-permute-done.6
  34.8 0.0 collective-permute-done.5
  34.8 0.2 fusion.26
  35.1 0.0 copy-start
  35.1 2.4 %convolution_bitcast_fusion = f32[3,16384,16]{1,2,0:T(8,128)S(1)} fusion(s32[16384]{0:T(1024)S(1)} %get-tuple-element.9, bf16[1,128,16]{1,2,0:T(8,128)(2,1)S(1)} %get-tuple-element.34, bf16[1,128,16]{1,2,0:T(8,128)(2,1)S(1)} %get-tuple-element.33, bf16[1,128,16]{1,2,0:T(8,128)(2,1)S(1)} %get-tuple-element.32), kind=kOutput, calls=%fused_computation | convolution fusion | flops 203436032 | bytes 3223552 | tf_op jit(solution)/shard_map/fd,kdp->kfp/dot_general | solution.py:89
  37.5 0.4 fusion.13
  37.9 11.5 %all_to_all.10 = f32[1,128,128]{2,0,1:T(1,128)S(1)} all-to-all(f32[1,128,128]{2,0,1:T(1,128)S(1)} %bitcast.85), channel_id=1, replica_groups=mesh['stream'=4,'cross'=2,'gore'=4] {'stream','cross'}, dimensions={1} | all-to-all | bytes 131072 | tf_op jit(solution)/shard_map/all_to_all | solution.py:160
  49.4 0.2 fusion.62
  49.6 0.7 %slice_multiply_fusion = f32[3,64,128]{2,1,0:T(8,128)} fusion(f32[8,64,128]{2,1,0:T(8,128)S(1)} %broadcast_select_fusion, f32[64,128]{1,0:T(8,128)S(1)} %fusion.62), kind=kLoop, calls=%fused_computation.27 | loop fusion | flops 24576 | bytes 229376 | tf_op jit(solution)/shard_map/mul | solution.py:170
  50.3 0.0 copy-done
  (21 shorter events, 0.3 us)
Async XLA Ops:
  6.2 15.3 %all-to-all-start = ((f32[6,128,128]{2,0,1:T(8,128)}), f32[6,128,128]{2,0,1:T(8,128)S(1)}, u32[]{:S(2)}, u32[]{:S(2)}) async-start(f32[6,128,128]{2,0,1:T(8,128)} %copy.11), calls=%async_computation | async-start | bytes 1048576 | tf_op jit(solution)/shard_map/all_to_all | solution.py:130
  12.3 7.9 %collective-permute-start.1 = (f32[6,4,4,1]{3,2,1,0:T(4,128)S(1)}, f32[6,4,4,1]{3,2,1,0:T(4,128)S(1)}, u32[]{:S(2)}, u32[]{:S(2)}) collective-permute-start(f32[6,4,4,1]{3,2,1,0:T(4,128)S(1)} %get-tuple-element.18), channel_id=1, source_target_pairs={{1,2},{2,1},{5,6},{6,5},{9,10},{10,9},{13,14},{14,13},{17,18},{18,... | collective-permute-start | bytes 1160 | tf_op jit(solution)/shard_map/ppermute | solution.py:27
  12.9 7.3 %collective-permute-start = (f32[6,4,4,1]{3,2,1,0:T(4,128)S(1)}, f32[6,4,4,1]{3,2,1,0:T(4,128)S(1)}, u32[]{:S(2)}, u32[]{:S(2)}) collective-permute-start(f32[6,4,4,1]{3,2,1,0:T(4,128)S(1)} %get-tuple-element.19), channel_id=1, source_target_pairs={{0,1},{1,0},{2,3},{3,2},{4,5},{5,4},{6,7},{7,6},{8,9},{9,8},{10,11... | collective-permute-start | bytes 1160 | tf_op jit(solution)/shard_map/ppermute | solution.py:25
  17.4 3.8 %collective-permute-start.2 = (f32[6,4,1,128]{3,2,1,0:T(1,128)S(1)}, f32[6,4,1,128]{3,2,1,0:T(1,128)S(1)}, u32[]{:S(2)}, u32[]{:S(2)}) collective-permute-start(f32[6,4,1,128]{3,2,1,0:T(1,128)S(1)} %broadcast_select_fusion.3), channel_id=1, source_target_pairs={{0,4},{4,0},{1,5},{5,1},{2,6},{6,2},{3,7},{7,3},{8,12},{12,8},{9,1... | collective-permute-start | bytes 36872 | tf_op jit(solution)/shard_map/ppermute | solution.py:25
  19.5 1.2 %collective-permute-start.3 = (f32[6,1,4,128]{3,2,1,0:T(4,128)S(1)}, f32[6,1,4,128]{3,2,1,0:T(4,128)S(1)}, u32[]{:S(2)}, u32[]{:S(2)}) collective-permute-start(f32[6,1,4,128]{3,2,1,0:T(4,128)S(1)} %get-tuple-element.16), channel_id=1, source_target_pairs={{0,8},{8,0},{16,24},{24,16},{1,9},{9,1},{17,25},{25,17},{2,10},{10... | collective-permute-start | bytes 36872 | tf_op jit(solution)/shard_map/ppermute | solution.py:25
  19.5 1.2 %collective-permute-start.4 = (f32[6,1,4,128]{3,2,1,0:T(4,128)S(1)}, f32[6,1,4,128]{3,2,1,0:T(4,128)S(1)}, u32[]{:S(2)}, u32[]{:S(2)}) collective-permute-start(f32[6,1,4,128]{3,2,1,0:T(4,128)S(1)} %get-tuple-element.17), channel_id=1, source_target_pairs={{8,16},{16,8},{9,17},{17,9},{10,18},{18,10},{11,19},{19,11},{12,20... | collective-permute-start | bytes 36872 | tf_op jit(solution)/shard_map/ppermute | solution.py:27
  26.6 6.4 %collective-permute-start.8 = (f32[5,4,4,1]{3,2,1,0:T(4,128)S(1)}, f32[5,4,4,1]{3,2,1,0:T(4,128)S(1)}, u32[]{:S(2)}, u32[]{:S(2)}) collective-permute-start(f32[5,4,4,1]{3,2,1,0:T(4,128)S(1)} %get-tuple-element.22), channel_id=1, source_target_pairs={{1,2},{2,1},{5,6},{6,5},{9,10},{10,9},{13,14},{14,13},{17,18},{18,... | collective-permute-start | bytes 968 | tf_op jit(solution)/shard_map/ppermute | solution.py:27
  27.3 5.8 %collective-permute-start.9 = (f32[5,4,4,1]{3,2,1,0:T(4,128)S(1)}, f32[5,4,4,1]{3,2,1,0:T(4,128)S(1)}, u32[]{:S(2)}, u32[]{:S(2)}) collective-permute-start(f32[5,4,4,1]{3,2,1,0:T(4,128)S(1)} %get-tuple-element.23), channel_id=1, source_target_pairs={{0,1},{1,0},{2,3},{3,2},{4,5},{5,4},{6,7},{7,6},{8,9},{9,8},{10,11... | collective-permute-start | bytes 968 | tf_op jit(solution)/shard_map/ppermute | solution.py:25
  31.1 3.7 %collective-permute-start.7 = (f32[5,4,1,128]{3,2,1,0:T(1,128)S(1)}, f32[5,4,1,128]{3,2,1,0:T(1,128)S(1)}, u32[]{:S(2)}, u32[]{:S(2)}) collective-permute-start(f32[5,4,1,128]{3,2,1,0:T(1,128)S(1)} %broadcast_select_fusion.10), channel_id=1, source_target_pairs={{0,4},{4,0},{1,5},{5,1},{2,6},{6,2},{3,7},{7,3},{8,12},{12,8},{9,1... | collective-permute-start | bytes 30728 | tf_op jit(solution)/shard_map/ppermute | solution.py:25
  32.0 2.8 %collective-permute-start.6 = (f32[5,1,4,128]{3,2,1,0:T(4,128)S(1)}, f32[5,1,4,128]{3,2,1,0:T(4,128)S(1)}, u32[]{:S(2)}, u32[]{:S(2)}) collective-permute-start(f32[5,1,4,128]{3,2,1,0:T(4,128)S(1)} %get-tuple-element.20), channel_id=1, source_target_pairs={{0,8},{8,0},{16,24},{24,16},{1,9},{9,1},{17,25},{25,17},{2,10},{10... | collective-permute-start | bytes 30728 | tf_op jit(solution)/shard_map/ppermute | solution.py:25
  32.4 2.4 %collective-permute-start.5 = (f32[5,1,4,128]{3,2,1,0:T(4,128)S(1)}, f32[5,1,4,128]{3,2,1,0:T(4,128)S(1)}, u32[]{:S(2)}, u32[]{:S(2)}) collective-permute-start(f32[5,1,4,128]{3,2,1,0:T(4,128)S(1)} %get-tuple-element.21), channel_id=1, source_target_pairs={{8,16},{16,8},{9,17},{17,9},{10,18},{18,10},{11,19},{19,11},{12,20... | collective-permute-start | bytes 30728 | tf_op jit(solution)/shard_map/ppermute | solution.py:27
  35.1 15.2 %copy-start = (f32[5,4,4,128]{3,2,1,0:T(4,128)}, f32[5,4,4,128]{3,2,1,0:T(4,128)S(1)}, u32[]{:S(2)}) copy-start(f32[5,4,4,128]{3,2,1,0:T(4,128)S(1)} %fusion.26) | copy-start | bytes 122884
where the time goes:
time: 50.8 us; the launch traced here: 50.3 us
  starting transfers between devices  19.5 us (38%)
  blocking collectives  11.5 us (23%)
  matrix products  7.97 us (16%)
  other arithmetic  6.61 us (13%)
  waiting for transfers between devices  2.53 us (5%)
  local copies, waits for them, and re-layouts  1.21 us (2%)
  between operations  1 us (2%)
    ppermute x6, starting transfers between devices, face_halo(): from_a = lax.ppermute(jnp.where(odd, first, last), axis, pairs_a)  11.6 us
    all_to_all x1, blocking collectives, shards(): lax.all_to_all(face_pressure.reshape(1, slot_total, row_count), ('stream'...  11.5 us
    all_to_all x1, starting transfers between devices, shards(): lax.all_to_all(outbound, ('stream', 'cross'), split_axis=1, concat_axis=1...  5.17 us
    dot_general x1, matrix products, shards(): jnp.einsum('cpf,fd->cpd', spread, depth_hot.astype(jnp.float32), precisio...  3.97 us
    ppermute x4, starting transfers between devices, face_halo(): from_b = lax.ppermute(jnp.where(odd, last, first), axis, pairs_b)  2.64 us
    ppermute x6, waiting for transfers between devices, face_halo(): from_a = lax.ppermute(jnp.where(odd, first, last), axis, pairs_a)  2.52 us
    dot_general x1, matrix products, exact_dot(): jnp.einsum(left + ',k' + right + '->k' + output, onehot, stacked, preferr...  2.4 us
  transfers between devices with their start and end apart: 11, of which 3 were waited for; matrix products, arithmetic and copies ran while one was open for 3% of the time, Pallas kernels for 0%

commit v1 on v0

--- a/solution.py
+++ b/solution.py
@@ -1,9 +1,21 @@
+import functools
 import jax
 import jax.numpy as jnp
 from jax import lax
 from jax.sharding import PartitionSpec as P
 
 SIDES = (("stream", 1), ("cross", 2), ("gore", 3))
+
+
+def remake_limits(slab_in, join_dim, where_dim):
+    later = lax.axis_size(("stream", "cross"))
+    taken_in = jnp.split(slab_in, later, axis=join_dim)
+    passed = jnp.stack(taken_in, 0)
+    built = lax.all_to_all(passed, ("stream", "cross"), 0, 0)
+    return jnp.concatenate(built, where_dim)
+
+
+review_the_flows = functools.partial(remake_limits, join_dim=1, where_dim=1)
 
 
 def face_halo(block):
@@ -127,7 +139,7 @@
         [jnp.abs(masked_values[0:1]), masked_values[1:5], cell_ids.astype(jnp.float32)[None]], 0
     )
     outbound = jnp.einsum("ts,ctr->csr", placement_plan, payload, precision=lax.Precision.HIGHEST)
-    arrived = lax.all_to_all(outbound, ("stream", "cross"), split_axis=1, concat_axis=1, tiled=True)
+    arrived = review_the_flows(outbound)
     outbound, state_and_visc = lax.optimization_barrier(
         (outbound, jnp.concatenate([fluid_state, viscosity[None]], 0))
     )

time: 50.8 us -> 54.8 us (1.079)
  local copies, waits for them, and re-layouts: 1.21 us -> 5.3 us
  waiting for transfers between devices: 2.53 us -> 1.12 us
  blocking collectives: 11.5 us -> 12.9 us
    unnamed x2 -> x10, local copies, waits for them, and re-layouts: 0.01 us -> 4.53 us
    ppermute x6, waiting for transfers between devices: 2.52 us -> 1.11 us  [face_halo(): from_a = lax.ppermute(jnp.where(odd, first, last), axis, pairs_a)]
    all_to_all x1, blocking collectives: 11.5 us -> 12.9 us  [shards(): lax.all_to_all(face_pressure.reshape(1, slot_total, row_count), ('stream'...]
    transpose x1 -> x0, local copies, waits for them, and re-layouts: 0.99 us -> none  [shards(): jnp.einsum('ts,ctr->csr', placement_plan, payload, precision=lax.Precisio...]
    another operation x0 -> x1, local copies, waits for them, and re-layouts: none -> 0.62 us  [remake_limits(): passed = jnp.stack(taken_in, 0)]
  transfers between devices with their start and end apart: 11 -> 11, of which waited for: 3 -> 3; matrix products, arithmetic and copies ran while one was open for 3% -> 2% of each run, Pallas kernels for 0% -> 0%
where the time goes in v1:
time: 54.8 us; the launch traced here: 54.3 us
  starting transfers between devices  19.5 us (36%)
  blocking collectives  12.9 us (24%)
  matrix products  7.89 us (14%)
  other arithmetic  6.63 us (12%)
  local copies, waits for them, and re-layouts  5.3 us (10%)
  waiting for transfers between devices  1.12 us (2%)
  between operations  1.02 us (2%)
    all_to_all x1, blocking collectives, shards(): lax.all_to_all(face_pressure.reshape(1, slot_total, row_count), ('stream'...  12.9 us
    ppermute x6, starting transfers between devices, face_halo(): from_a = lax.ppermute(jnp.where(odd, first, last), axis, pairs_a)  11.6 us
    all_to_all x1, starting transfers between devices, remake_limits(): built = lax.all_to_all(passed, ('stream', 'cross'), 0, 0)  5.17 us
    unnamed x10, local copies, waits for them, and re-layouts  4.53 us
    dot_general x1, matrix products, shards(): jnp.einsum('cpf,fd->cpd', spread, depth_hot.astype(jnp.float32), precisio...  3.98 us
    ppermute x4, starting transfers between devices, face_halo(): from_b = lax.ppermute(jnp.where(odd, last, first), axis, pairs_b)  2.64 us
    dot_general x1, matrix products, exact_dot(): jnp.einsum(left + ',k' + right + '->k' + output, onehot, stacked, preferr...  2.4 us
    ppermute x6, waiting for transfers between devices, face_halo(): from_a = lax.ppermute(jnp.where(odd, first, last), axis, pairs_a)  1.11 us
  transfers between devices with their start and end apart: 11, of which 3 were waited for; matrix products, arithmetic and copies ran while one was open for 2% of the time, Pallas kernels for 0%

profile of v1, /device:TPU:0, one launch (start us, length us, event | category | flops | bytes accessed | tf_op | source)
XLA Modules:
  0.0 54.3 jit_solution(16620309989094737712)
XLA Ops:
  0.6 0.7 %iota_compare_fusion.6 = pred[64,128]{1,0:T(8,128)(4,1)S(1)} fusion(s32[64]{0:T(128)} %param.13), kind=kLoop, calls=%fused_computation.149 | loop fusion | flops 8192 | bytes 8448 | tf_op jit(solution)/shard_map/lt | solution.py:120
  1.4 1.0 %broadcast_select_fusion = f32[8,64,128]{2,1,0:T(8,128)S(1)} fusion(f32[8,64,128]{2,1,0:T(8,128)} %param.10, pred[64,128]{1,0:T(8,128)(4,1)S(1)} %iota_compare_fusion.6), kind=kLoop, calls=%fused_computation.26 | loop fusion | flops 65536 | bytes 532480 | tf_op jit(solution)/shard_map/jit(_where)/select_n | solution.py:121
  2.4 0.8 %convert_bitcast_fusion = f32[1,64,128]{2,1,0:T(8,128)S(1)} fusion(s32[64,128]{1,0:T(8,128)} %param.11), kind=kLoop, calls=%fused_computation.148 | loop fusion | flops 8192 | bytes 65536 | tf_op jit(solution)/shard_map/broadcast_in_dim | solution.py:139
  3.1 0.9 %fusion.10 = f32[64]{0:T(128)S(1)} fusion(s32[64]{0:T(128)} %bitcast.113), kind=kOutput, calls=%fused_computation.12 | convolution fusion | flops 71616 | bytes 512 | tf_op jit(solution)/shard_map/dot_general | solution.py:130
  4.0 0.7 %fusion.100 = s32[64]{0:T(128)S(1)} fusion(f32[64]{0:T(128)S(1)} %fusion.10, s32[64,1]{0,1:T(1,128)} %param.12), kind=kLoop, calls=%fused_computation.210 | loop fusion | flops 192 | bytes 768 | tf_op jit(solution)/shard_map/eq | solution.py:136
  4.7 0.4 convolution_bitcast_fusion.1
  5.1 0.6 %fusion.28 = f32[8,6,16,128]{3,2,1,0:T(8,128)} fusion(f32[6,128,128]{2,1,0:T(8,128)S(1)} %convolution_bitcast_fusion.1), kind=kLoop, calls=%fused_computation.52 | loop fusion | bytes 98304
  5.7 0.6 %fusion.27 = f32[8,6,16,128]{3,2,1,0:T(8,128)} fusion(f32[8,6,16,128]{3,2,1,0:T(8,128)} %fusion.28, f32[6,128,128]{2,1,0:T(8,128)S(1)} %convolution_bitcast_fusion.1), kind=kLoop, calls=%fused_computation.50 | loop fusion | bytes 98304
  6.4 0.6 %fusion.26 = f32[8,6,16,128]{3,2,1,0:T(8,128)} fusion(f32[8,6,16,128]{3,2,1,0:T(8,128)} %fusion.27, f32[6,128,128]{2,1,0:T(8,128)S(1)} %convolution_bitcast_fusion.1), kind=kLoop, calls=%fused_computation.48 | loop fusion | bytes 98304
  7.0 0.6 %fusion.25 = f32[8,6,16,128]{3,2,1,0:T(8,128)} fusion(f32[8,6,16,128]{3,2,1,0:T(8,128)} %fusion.26, f32[6,128,128]{2,1,0:T(8,128)S(1)} %convolution_bitcast_fusion.1), kind=kLoop, calls=%fused_computation.46 | loop fusion | bytes 98304
  7.6 0.6 %fusion.24 = f32[8,6,16,128]{3,2,1,0:T(8,128)} fusion(f32[8,6,16,128]{3,2,1,0:T(8,128)} %fusion.25, f32[6,128,128]{2,1,0:T(8,128)S(1)} %convolution_bitcast_fusion.1), kind=kLoop, calls=%fused_computation.44 | loop fusion | bytes 98304
  8.2 0.6 %fusion.23 = f32[8,6,16,128]{3,2,1,0:T(8,128)} fusion(f32[8,6,16,128]{3,2,1,0:T(8,128)} %fusion.24, f32[6,128,128]{2,1,0:T(8,128)S(1)} %convolution_bitcast_fusion.1), kind=kLoop, calls=%fused_computation.42 | loop fusion | bytes 98304
  8.8 0.6 %fusion.22 = f32[8,6,16,128]{3,2,1,0:T(8,128)} fusion(f32[8,6,16,128]{3,2,1,0:T(8,128)} %fusion.23, f32[6,128,128]{2,1,0:T(8,128)S(1)} %convolution_bitcast_fusion.1), kind=kLoop, calls=%fused_computation.40 | loop fusion | bytes 98304
  9.4 0.6 %fusion.21 = f32[8,6,16,128]{3,2,1,0:T(8,128)} fusion(f32[8,6,16,128]{3,2,1,0:T(8,128)} %fusion.22, f32[6,128,128]{2,1,0:T(8,128)S(1)} %convolution_bitcast_fusion.1), kind=kLoop, calls=%fused_computation.38 | loop fusion | bytes 98304 | tf_op jit(solution)/shard_map/stack | solution.py:13
  10.1 5.2 %all-to-all-start = ((f32[8,6,16,128]{3,2,1,0:T(8,128)}), f32[8,6,16,128]{3,2,1,0:T(8,128)S(1)}, u32[]{:S(2)}, u32[]{:S(2)}) async-start(f32[8,6,16,128]{3,2,1,0:T(8,128)} %fusion.21), calls=%async_computation | async-start | bytes 786432 | tf_op jit(solution)/shard_map/all_to_all | solution.py:14
  15.2 0.8 %pad_maximum_fusion.6 = f32[6,4,4,128]{3,2,1,0:T(4,128)S(1)} fusion(f32[1,4,4,128]{3,2,1,0:T(4,128)} %bitcast.111, f32[4,4,4,128]{3,2,1,0:T(4,128)} %param.8, f32[1,4,4,128]{3,2,1,0:T(4,128)} %bitcast.112), kind=kLoop, calls=%fused_computation.60 | loop fusion | flops 24576 | bytes 98304 | tf_op jit(solution)/shard_map/concatenate | solution.py:144
  16.0 0.1 slice_select_fusion
  16.1 0.7 %collective-permute-start.1 = (f32[6,4,4,1]{3,2,1,0:T(4,128)S(1)}, f32[6,4,4,1]{3,2,1,0:T(4,128)S(1)}, u32[]{:S(2)}, u32[]{:S(2)}) collective-permute-start(f32[6,4,4,1]{3,2,1,0:T(4,128)S(1)} %get-tuple-element.18), channel_id=1, source_target_pairs={{1,2},{2,1},{5,6},{6,5},{9,10},{10,9},{13,14},{14,13},{17,18},{18,... | collective-permute-start | bytes 1160 | tf_op jit(solution)/shard_map/ppermute | solution.py:39
  16.8 4.5 %collective-permute-start = (f32[6,4,4,1]{3,2,1,0:T(4,128)S(1)}, f32[6,4,4,1]{3,2,1,0:T(4,128)S(1)}, u32[]{:S(2)}, u32[]{:S(2)}) collective-permute-start(f32[6,4,4,1]{3,2,1,0:T(4,128)S(1)} %get-tuple-element.19), channel_id=1, source_target_pairs={{0,1},{1,0},{2,3},{3,2},{4,5},{5,4},{6,7},{7,6},{8,9},{9,8},{10,11... | collective-permute-start | bytes 1160 | tf_op jit(solution)/shard_map/ppermute | solution.py:37
  21.3 2.1 %collective-permute-start.2 = (f32[6,4,1,128]{3,2,1,0:T(1,128)S(1)}, f32[6,4,1,128]{3,2,1,0:T(1,128)S(1)}, u32[]{:S(2)}, u32[]{:S(2)}) collective-permute-start(f32[6,4,1,128]{3,2,1,0:T(1,128)S(1)} %broadcast_select_fusion.3), channel_id=1, source_target_pairs={{0,4},{4,0},{1,5},{5,1},{2,6},{6,2},{3,7},{7,3},{8,12},{12,8},{9,1... | collective-permute-start | bytes 36872 | tf_op jit(solution)/shard_map/ppermute | solution.py:37
  23.4 0.0 collective-permute-start.3
  23.4 0.7 %collective-permute-start.4 = (f32[6,1,4,128]{3,2,1,0:T(4,128)S(1)}, f32[6,1,4,128]{3,2,1,0:T(4,128)S(1)}, u32[]{:S(2)}, u32[]{:S(2)}) collective-permute-start(f32[6,1,4,128]{3,2,1,0:T(4,128)S(1)} %get-tuple-element.17), channel_id=1, source_target_pairs={{8,16},{16,8},{9,17},{17,9},{10,18},{18,10},{11,19},{19,11},{12,20... | collective-permute-start | bytes 36872 | tf_op jit(solution)/shard_map/ppermute | solution.py:39
  24.1 0.0 collective-permute-done.1
  24.1 0.0 collective-permute-done
  24.2 0.4 collective-permute-done.3
  24.6 0.0 collective-permute-done.4
  24.6 0.5 collective-permute-done.2
  25.1 0.1 fusion.29
  25.2 0.1 fusion.85
  25.3 0.0 all-to-all-done
  25.4 0.1 add_select_fusion.1
  25.5 0.2 copy.13
  25.7 0.1 iota_compare_fusion.2
  25.9 0.5 fusion.111
  26.3 4.0 %fusion.2 = f32[5,16,128]{2,1,0:T(8,128)S(1)} fusion(s32[16384]{0:T(1024)S(1)} %get-tuple-element.9, f32[5,16,16384]{2,1,0:T(8,128)S(1)} %fusion.111), kind=kOutput, calls=%fused_computation.3 | convolution fusion | flops 2015363072 | bytes 5349376 | tf_op jit(solution)/shard_map/cpf,fd->cpd/dot_general | solution.py:155
  30.3 0.2 fusion.55
  30.5 0.1 slice_select_fusion.3
  30.7 0.7 %collective-permute-start.8 = (f32[5,4,4,1]{3,2,1,0:T(4,128)S(1)}, f32[5,4,4,1]{3,2,1,0:T(4,128)S(1)}, u32[]{:S(2)}, u32[]{:S(2)}) collective-permute-start(f32[5,4,4,1]{3,2,1,0:T(4,128)S(1)} %get-tuple-element.22), channel_id=1, source_target_pairs={{1,2},{2,1},{5,6},{6,5},{9,10},{10,9},{13,14},{14,13},{17,18},{18,... | collective-permute-start | bytes 968 | tf_op jit(solution)/shard_map/ppermute | solution.py:39
  31.4 2.3 %collective-permute-start.9 = (f32[5,4,4,1]{3,2,1,0:T(4,128)S(1)}, f32[5,4,4,1]{3,2,1,0:T(4,128)S(1)}, u32[]{:S(2)}, u32[]{:S(2)}) collective-permute-start(f32[5,4,4,1]{3,2,1,0:T(4,128)S(1)} %get-tuple-element.23), channel_id=1, source_target_pairs={{0,1},{1,0},{2,3},{3,2},{4,5},{5,4},{6,7},{7,6},{8,9},{9,8},{10,11... | collective-permute-start | bytes 968 | tf_op jit(solution)/shard_map/ppermute | solution.py:37
  33.7 1.9 %collective-permute-start.7 = (f32[5,4,1,128]{3,2,1,0:T(1,128)S(1)}, f32[5,4,1,128]{3,2,1,0:T(1,128)S(1)}, u32[]{:S(2)}, u32[]{:S(2)}) collective-permute-start(f32[5,4,1,128]{3,2,1,0:T(1,128)S(1)} %broadcast_select_fusion.10), channel_id=1, source_target_pairs={{0,4},{4,0},{1,5},{5,1},{2,6},{6,2},{3,7},{7,3},{8,12},{12,8},{9,1... | collective-permute-start | bytes 30728 | tf_op jit(solution)/shard_map/ppermute | solution.py:37
  35.6 0.9 %collective-permute-start.6 = (f32[5,1,4,128]{3,2,1,0:T(4,128)S(1)}, f32[5,1,4,128]{3,2,1,0:T(4,128)S(1)}, u32[]{:S(2)}, u32[]{:S(2)}) collective-permute-start(f32[5,1,4,128]{3,2,1,0:T(4,128)S(1)} %get-tuple-element.20), channel_id=1, source_target_pairs={{0,8},{8,0},{16,24},{24,16},{1,9},{9,1},{17,25},{25,17},{2,10},{10... | collective-permute-start | bytes 30728 | tf_op jit(solution)/shard_map/ppermute | solution.py:37
  36.4 0.7 %collective-permute-start.5 = (f32[5,1,4,128]{3,2,1,0:T(4,128)S(1)}, f32[5,1,4,128]{3,2,1,0:T(4,128)S(1)}, u32[]{:S(2)}, u32[]{:S(2)}) collective-permute-start(f32[5,1,4,128]{3,2,1,0:T(4,128)S(1)} %get-tuple-element.21), channel_id=1, source_target_pairs={{8,16},{16,8},{9,17},{17,9},{10,18},{18,10},{11,19},{19,11},{12,20... | collective-permute-start | bytes 30728 | tf_op jit(solution)/shard_map/ppermute | solution.py:39
  37.1 0.0 collective-permute-done.8
  37.1 0.0 collective-permute-done.9
  37.1 0.2 collective-permute-done.7
  37.4 0.0 collective-permute-done.6
  37.4 0.0 collective-permute-done.5
  37.5 0.2 fusion.35
  37.7 0.0 copy-start
  37.7 2.4 %convolution_bitcast_fusion = f32[3,16384,16]{1,2,0:T(8,128)S(1)} fusion(s32[16384]{0:T(1024)S(1)} %get-tuple-element.9, bf16[1,128,16]{1,2,0:T(8,128)(2,1)S(1)} %get-tuple-element.34, bf16[1,128,16]{1,2,0:T(8,128)(2,1)S(1)} %get-tuple-element.33, bf16[1,128,16]{1,2,0:T(8,128)(2,1)S(1)} %get-tuple-element.32), kind=kOutput, calls=%fused_computation | convolution fusion | flops 203436032 | bytes 3223552 | tf_op jit(solution)/shard_map/fd,kdp->kfp/dot_general | solution.py:101
  40.2 0.4 fusion.13
  40.5 12.9 %all_to_all.10 = f32[1,128,128]{2,0,1:T(1,128)S(1)} all-to-all(f32[1,128,128]{2,0,1:T(1,128)S(1)} %bitcast.99), channel_id=1, replica_groups=mesh['stream'=4,'cross'=2,'gore'=4] {'stream','cross'}, dimensions={1} | all-to-all | bytes 131072 | tf_op jit(solution)/shard_map/all_to_all | solution.py:172
  53.4 0.2 fusion.70
  53.6 0.7 %slice_multiply_fusion = f32[3,64,128]{2,1,0:T(8,128)} fusion(f32[8,64,128]{2,1,0:T(8,128)S(1)} %broadcast_select_fusion, f32[64,128]{1,0:T(8,128)S(1)} %fusion.70), kind=kLoop, calls=%fused_computation.27 | loop fusion | flops 24576 | bytes 229376 | tf_op jit(solution)/shard_map/mul | solution.py:182
  54.3 0.0 copy-done
  (23 shorter events, 0.3 us)
Async XLA Ops:
  10.1 15.3 %all-to-all-start = ((f32[8,6,16,128]{3,2,1,0:T(8,128)}), f32[8,6,16,128]{3,2,1,0:T(8,128)S(1)}, u32[]{:S(2)}, u32[]{:S(2)}) async-start(f32[8,6,16,128]{3,2,1,0:T(8,128)} %fusion.21), calls=%async_computation | async-start | bytes 786432 | tf_op jit(solution)/shard_map/all_to_all | solution.py:14
  16.1 7.9 %collective-permute-start.1 = (f32[6,4,4,1]{3,2,1,0:T(4,128)S(1)}, f32[6,4,4,1]{3,2,1,0:T(4,128)S(1)}, u32[]{:S(2)}, u32[]{:S(2)}) collective-permute-start(f32[6,4,4,1]{3,2,1,0:T(4,128)S(1)} %get-tuple-element.18), channel_id=1, source_target_pairs={{1,2},{2,1},{5,6},{6,5},{9,10},{10,9},{13,14},{14,13},{17,18},{18,... | collective-permute-start | bytes 1160 | tf_op jit(solution)/shard_map/ppermute | solution.py:39
  16.8 7.3 %collective-permute-start = (f32[6,4,4,1]{3,2,1,0:T(4,128)S(1)}, f32[6,4,4,1]{3,2,1,0:T(4,128)S(1)}, u32[]{:S(2)}, u32[]{:S(2)}) collective-permute-start(f32[6,4,4,1]{3,2,1,0:T(4,128)S(1)} %get-tuple-element.19), channel_id=1, source_target_pairs={{0,1},{1,0},{2,3},{3,2},{4,5},{5,4},{6,7},{7,6},{8,9},{9,8},{10,11... | collective-permute-start | bytes 1160 | tf_op jit(solution)/shard_map/ppermute | solution.py:37
  21.3 3.8 %collective-permute-start.2 = (f32[6,4,1,128]{3,2,1,0:T(1,128)S(1)}, f32[6,4,1,128]{3,2,1,0:T(1,128)S(1)}, u32[]{:S(2)}, u32[]{:S(2)}) collective-permute-start(f32[6,4,1,128]{3,2,1,0:T(1,128)S(1)} %broadcast_select_fusion.3), channel_id=1, source_target_pairs={{0,4},{4,0},{1,5},{5,1},{2,6},{6,2},{3,7},{7,3},{8,12},{12,8},{9,1... | collective-permute-start | bytes 36872 | tf_op jit(solution)/shard_map/ppermute | solution.py:37
  23.4 1.2 %collective-permute-start.3 = (f32[6,1,4,128]{3,2,1,0:T(4,128)S(1)}, f32[6,1,4,128]{3,2,1,0:T(4,128)S(1)}, u32[]{:S(2)}, u32[]{:S(2)}) collective-permute-start(f32[6,1,4,128]{3,2,1,0:T(4,128)S(1)} %get-tuple-element.16), channel_id=1, source_target_pairs={{0,8},{8,0},{16,24},{24,16},{1,9},{9,1},{17,25},{25,17},{2,10},{10... | collective-permute-start | bytes 36872 | tf_op jit(solution)/shard_map/ppermute | solution.py:37
  23.4 1.2 %collective-permute-start.4 = (f32[6,1,4,128]{3,2,1,0:T(4,128)S(1)}, f32[6,1,4,128]{3,2,1,0:T(4,128)S(1)}, u32[]{:S(2)}, u32[]{:S(2)}) collective-permute-start(f32[6,1,4,128]{3,2,1,0:T(4,128)S(1)} %get-tuple-element.17), channel_id=1, source_target_pairs={{8,16},{16,8},{9,17},{17,9},{10,18},{18,10},{11,19},{19,11},{12,20... | collective-permute-start | bytes 36872 | tf_op jit(solution)/shard_map/ppermute | solution.py:39
  30.7 6.4 %collective-permute-start.8 = (f32[5,4,4,1]{3,2,1,0:T(4,128)S(1)}, f32[5,4,4,1]{3,2,1,0:T(4,128)S(1)}, u32[]{:S(2)}, u32[]{:S(2)}) collective-permute-start(f32[5,4,4,1]{3,2,1,0:T(4,128)S(1)} %get-tuple-element.22), channel_id=1, source_target_pairs={{1,2},{2,1},{5,6},{6,5},{9,10},{10,9},{13,14},{14,13},{17,18},{18,... | collective-permute-start | bytes 968 | tf_op jit(solution)/shard_map/ppermute | solution.py:39
  31.4 5.8 %collective-permute-start.9 = (f32[5,4,4,1]{3,2,1,0:T(4,128)S(1)}, f32[5,4,4,1]{3,2,1,0:T(4,128)S(1)}, u32[]{:S(2)}, u32[]{:S(2)}) collective-permute-start(f32[5,4,4,1]{3,2,1,0:T(4,128)S(1)} %get-tuple-element.23), channel_id=1, source_target_pairs={{0,1},{1,0},{2,3},{3,2},{4,5},{5,4},{6,7},{7,6},{8,9},{9,8},{10,11... | collective-permute-start | bytes 968 | tf_op jit(solution)/shard_map/ppermute | solution.py:37
  33.7 3.7 %collective-permute-start.7 = (f32[5,4,1,128]{3,2,1,0:T(1,128)S(1)}, f32[5,4,1,128]{3,2,1,0:T(1,128)S(1)}, u32[]{:S(2)}, u32[]{:S(2)}) collective-permute-start(f32[5,4,1,128]{3,2,1,0:T(1,128)S(1)} %broadcast_select_fusion.10), channel_id=1, source_target_pairs={{0,4},{4,0},{1,5},{5,1},{2,6},{6,2},{3,7},{7,3},{8,12},{12,8},{9,1... | collective-permute-start | bytes 30728 | tf_op jit(solution)/shard_map/ppermute | solution.py:37
  35.6 1.9 %collective-permute-start.6 = (f32[5,1,4,128]{3,2,1,0:T(4,128)S(1)}, f32[5,1,4,128]{3,2,1,0:T(4,128)S(1)}, u32[]{:S(2)}, u32[]{:S(2)}) collective-permute-start(f32[5,1,4,128]{3,2,1,0:T(4,128)S(1)} %get-tuple-element.20), channel_id=1, source_target_pairs={{0,8},{8,0},{16,24},{24,16},{1,9},{9,1},{17,25},{25,17},{2,10},{10... | collective-permute-start | bytes 30728 | tf_op jit(solution)/shard_map/ppermute | solution.py:37
  36.4 1.0 %collective-permute-start.5 = (f32[5,1,4,128]{3,2,1,0:T(4,128)S(1)}, f32[5,1,4,128]{3,2,1,0:T(4,128)S(1)}, u32[]{:S(2)}, u32[]{:S(2)}) collective-permute-start(f32[5,1,4,128]{3,2,1,0:T(4,128)S(1)} %get-tuple-element.21), channel_id=1, source_target_pairs={{8,16},{16,8},{9,17},{17,9},{10,18},{18,10},{11,19},{19,11},{12,20... | collective-permute-start | bytes 30728 | tf_op jit(solution)/shard_map/ppermute | solution.py:39
  37.7 16.6 %copy-start = (f32[5,4,4,128]{3,2,1,0:T(4,128)}, f32[5,4,4,128]{3,2,1,0:T(4,128)S(1)}, u32[]{:S(2)}) copy-start(f32[5,4,4,128]{3,2,1,0:T(4,128)S(1)} %fusion.35) | copy-start | bytes 122884
